TPU v7x, 256 devices: a whole 4x4x8 slice. The times are simulated.
256 devices in a mesh: gx: 8 (over x, core), gy: 32 (over y, z).
Axes of the slice: x: 4, y: 4, z: 8, core: 2. Of those that a mesh axis runs over, the one named last changes fastest.
Arguments:
- cells: bfloat16 [256, 1048576], P(None, ('gx', 'gy')), may hold values from -25 to 25
- send_index: int32 [8192, 2], P(('gx', 'gy')), may hold values from 0 to 31
- send_count: int32 [8192], P(('gx', 'gy')), may hold values from 1 to 2, as said below
- prolong_block: int32 [8192, 4], P(('gx', 'gy')), may hold values from 0 to 63, as said below
- prolong_level: int32 [8192, 4], P(('gx', 'gy')), may hold values from 0 to 3
- prolong_maps: bfloat16 [4, 128, 512], replicated, may hold values from -0.25 to 0.25
Outputs:
- factor: float32 [256, 256], replicated
- modes: float32 [128, 4194304], P(None, ('gx', 'gy'))
Inputs may be any that keep to these rules, and one draw needn't show every extreme that they name: `send_count`: every sender and owner pair uses 1 to 2 slots; some pair uses all 2. `prolong_block`: the first slot feeding each brick is slot 0 of some sender, a multiple of 2.
All inputs are finite; a program needn't handle non-finite values.
Results may differ from a plain program's by a relative error of at most 0.0041.
Values may be sent and summed in bfloat16 or wider, within the bound.
No kernel may reach another device: no remote copies, remote signals or barrier semaphores. Data moves between devices by JAX's collectives and lax.ppermute only.
A program may use at most 128 MiB of HBM per device.

v0:
```python
import jax
import jax.numpy as jnp
from jax import lax
from jax.sharding import PartitionSpec as P

RANK = 128
BLK = 128


def from_partner(value, axis, bit):
    mask = 2**bit
    pairs = [(source, source ^ mask) for source in range(lax.axis_size(axis))]
    return lax.ppermute(value, axis, pairs)


def lift(received, blocks, levels, maps):
    picked = jnp.take(received, blocks, axis=1)
    chosen = jnp.take(maps, levels, axis=0)
    lifted = jnp.einsum("sbnc,bncd->sbd", picked, chosen, preferred_element_type=jnp.float32)
    return lifted.reshape(lifted.shape[0], -1).astype(jnp.bfloat16)


def combined(factor, other):
    mine = jnp.dot(factor, factor.T, precision=lax.Precision.HIGHEST)
    theirs = jnp.dot(other, other.T, precision=lax.Precision.HIGHEST)
    return jnp.linalg.cholesky(mine + theirs)


def body(cells, send_index, send_count, prolong_block, prolong_level, prolong_maps):
    snaps = cells.shape[0]
    local = cells.reshape(snaps, -1, BLK)
    peers, slots = send_index.shape
    outgoing = jnp.take(local, send_index.reshape(-1), axis=1)
    live = (jnp.arange(slots, dtype=jnp.int32)[None, :] < send_count[:, None]).reshape(-1)
    outgoing = outgoing * live[None, :, None].astype(jnp.bfloat16)
    received = lax.all_to_all(outgoing, "gy", split_axis=1, concat_axis=1, tiled=True)
    bricks = lift(received, prolong_block, prolong_level, prolong_maps)
    gram = lax.dot_general(
        bricks, bricks, (((1,), (1,)), ((), ())), preferred_element_type=jnp.float32
    )
    total_cells = lax.axis_size("gx") * lax.axis_size("gy") * bricks.shape[1]
    gram = lax.psum(gram, ("gx", "gy"))
    covariance = gram / total_cells
    factor = jnp.linalg.cholesky(covariance)
    kept = RANK
    modes = lax.linalg.triangular_solve(
        factor[:kept, :kept], bricks[:kept].astype(jnp.float32), left_side=True, lower=True
    )
    return (factor, modes)


def solution(mesh):
    in_specs = (
        P(None, ("gx", "gy")),
        P(("gx", "gy"), None),
        P(("gx", "gy")),
        P(("gx", "gy"), None),
        P(("gx", "gy"), None),
        P(),
    )
    out_specs = (P(), P(None, ("gx", "gy")))
    return jax.shard_map(body, mesh=mesh, in_specs=in_specs, out_specs=out_specs, check_vma=False)
```

profile of v0, /device:TPU:2, one launch (start us, length us, event | category | flops | bytes accessed | tf_op | source)
XLA Modules:
  0.0 478.6 jit_solution(10285981647548982762)
XLA Ops:
  7.2 0.0 copy-start
  7.2 0.0 copy-start.5
  7.2 0.8 copy.35
  8.0 0.1 reshape.97
  8.1 0.1 reshape.95
  8.3 4.1 copy.36
  12.3 3.2 copy.38
  15.6 0.0 copy-done.5
  15.6 0.1 fusion.20
  15.6 0.1 reshape.98
  15.8 3.1 gather_fusion.1
  18.9 0.0 copy-start.4
  18.9 4.7 multiply_bitcast_fusion
  23.6 11.6 %all-to-all-start = ((bf16[256,64,128]{2,0,1:T(8,128)(2,1)}), bf16[256,64,128]{2,0,1:T(8,128)(2,1)}, u32[]{:S(2)}, u32[]{:S(2)}) async-start(bf16[256,64,128]{2,0,1:T(8,128)(2,1)} %multiply_bitcast_fusion), calls=%async_computation | async-start | bytes 8388608 | tf_op jit(solution)/shard_map/all_to_all | solution.py:36
  35.2 0.0 all-reduce.3.cloned.1.call-start
  35.3 0.0 copy-done.4
  35.3 0.1 copy.39
  35.4 0.1 reshape.117
  35.5 0.0 copy-done.3
  35.5 0.1 copy.32
  35.6 0.1 reshape.101
  35.7 0.0 copy-done
  35.7 8.1 %gather_fusion = bf16[128,128,512]{2,1,0:T(8,128)(2,1)} fusion(bf16[4,128,512]{2,1,0:T(8,128)(2,1)S(1)} %copy-done, s32[1024]{0:T(1024)S(1)} %pad_clamp_fusion.2), kind=kCustom, calls=%fused_computation | custom fusion | bytes 33554944 | tf_op jit(solution)/shard_map/jit(_take)/gather | solution.py:18
  43.9 22.6 %copy.33 = bf16[32,4,128,512]{2,3,1,0:T(8,128)(2,1)} copy(bf16[32,4,128,512]{3,2,1,0:T(8,128)(2,1)} %bitcast.43) | data formatting | bytes 33554432 | tf_op jit(solution)/shard_map/jit(_take)/gather | solution.py:18
  66.5 0.1 copy.31
  66.6 0.1 copy.34
  66.7 65.5 %all-to-all-done = bf16[256,64,128]{2,0,1:T(8,128)(2,1)} async-done(((bf16[256,64,128]{2,0,1:T(8,128)(2,1)}), bf16[256,64,128]{2,0,1:T(8,128)(2,1)}, u32[]{:S(2)}, u32[]{:S(2)}) %all-to-all-start) | async-done | bytes 4194336 | tf_op jit(solution)/shard_map/all_to_all | solution.py:36
  132.2 8.9 %gather_fusion.2 = bf16[128,256,128]{2,1,0:T(8,128)(2,1)} fusion(bf16[256,64,128]{2,0,1:T(8,128)(2,1)} %all-to-all-done, s32[1024]{0:T(1024)S(1)} %pad_clamp_fusion), kind=kCustom, calls=%fused_computation.2 | custom fusion | bytes 16777728 | tf_op jit(solution)/shard_map/jit(_take)/gather | solution.py:17
  141.1 12.8 %fusion.3 = bf16[256,32,512]{0,2,1:T(8,128)(2,1)} fusion(bf16[32,4,256,128]{3,2,1,0:T(8,128)(2,1)} %bitcast.45, pred[32,4]{1,0:T(8,128)(4,1)S(1)} %copy.34, bf16[32,4,128,512]{2,3,1,0:T(8,128)(2,1)} %copy.33, pred[32,4]{1,0:T(8,128)(4,1)S(1)} %copy.31), kind=kOutput, calls=%fused_computation.7 | convolution fusion | flops 4311744512 | bytes 33554688 | tf_op jit(solution)/shard_map/sbnc,bncd->sbd/dot_general | solution.py:19
  154.0 9.8 %convolution_bitcast_fusion = f32[256,256]{0,1:T(8,128)} fusion(bf16[256,32,512]{0,2,1:T(8,128)(2,1)} %fusion.3), kind=kOutput, calls=%fused_computation.14 | convolution fusion | flops 2147483648 | bytes 8650752 | tf_op jit(solution)/shard_map/dot_general | solution.py:38
  163.8 0.0 all-reduce.3.cloned.1.call-update
  163.8 0.0 copy-start.1
  163.8 4.6 triangular_solve.20
  168.5 246.3 %all-reduce.3.cloned.1.call-done = f32[256,256]{0,1:T(8,128)} async-done(((f32[256,256]{0,1:T(8,128)}), f32[256,256]{0,1:T(8,128)}) %all-reduce.3.cloned.1.call-update) | async-done | bytes 262160 | tf_op jit(solution)/shard_map/psum | solution.py:42
  414.7 1.0 broadcast_multiply_fusion
  415.7 0.1 copy.43
  415.8 1.0 fusion.13
  416.9 11.7 %cholesky.53 = f32[128,128]{1,0:T(8,128)S(1)} custom-call(f32[128,128]{1,0:T(8,128)S(1)} %cholesky.124), custom_call_target="Cholesky" | custom-call | tf_op jit(solution)/shard_map/jit(cholesky)/cholesky | solution.py:44
  428.6 9.8 %custom-call.14 = f32[1,128,128]{1,2,0:T(8,128)S(1)} custom-call(f32[1,128,128]{2,1,0:T(8,128)S(1)} %get-tuple-element.5), custom_call_target="InvertDiagBlocksLowerTriangular" | custom-call | tf_op jit(solution)/shard_map/jit(cholesky)/cholesky | solution.py:44
  438.4 0.2 constant_dynamic-update-slice_fusion.1
  438.7 0.3 convolution_subtract_fusion
  438.9 11.9 %cholesky.111 = f32[128,128]{1,0:T(8,128)S(1)} custom-call(f32[128,128]{1,0:T(8,128)S(1)} %convolution_subtract_fusion), custom_call_target="Cholesky" | custom-call | tf_op jit(solution)/shard_map/jit(cholesky)/cholesky | solution.py:44
  450.9 0.6 compare_reduce_fusion
  452.9 0.0 copy-start.2
  452.9 9.8 %custom-call.15 = f32[1,128,128]{1,2,0:T(8,128)S(1)} custom-call(f32[1,128,128]{2,1,0:T(8,128)S(1)} %fusion.14), custom_call_target="InvertDiagBlocksLowerTriangular" | custom-call | tf_op jit(solution)/shard_map/triangular_solve | solution.py:46
  462.7 9.1 %fusion.17 = f32[128,16384]{1,0:T(8,128)} fusion(bf16[128,16384]{0,1:T(8,128)(2,1)} %bitcast.44, f32[1,128,128]{1,2,0:T(8,128)S(1)} %custom-call.15), kind=kOutput, calls=%fused_computation.25 | convolution fusion | flops 3221225472 | bytes 12648448 | tf_op jit(solution)/shard_map/triangular_solve | solution.py:46
  471.8 0.0 copy-done.2
  471.8 0.0 copy-done.1
  (16 shorter events, 0.2 us)
Async XLA Ops:
  7.2 28.5 %copy-start = (bf16[4,128,512]{2,1,0:T(8,128)(2,1)S(1)}, bf16[4,128,512]{2,1,0:T(8,128)(2,1)}, u32[]{:S(2)}) copy-start(bf16[4,128,512]{2,1,0:T(8,128)(2,1)} %param.11) | copy-start | bytes 1572868
  7.2 8.4 %copy-start.5 = (s32[32]{0:T(128)S(1)}, s32[32]{0:T(128)}, u32[]{:S(2)}) copy-start(s32[32]{0:T(128)} %param.8) | copy-start | bytes 388
  18.9 16.4 %copy-start.4 = (s32[32,4]{0,1:T(4,128)S(1)}, s32[32,4]{0,1:T(4,128)}, u32[]{:S(2)}) copy-start(s32[32,4]{0,1:T(4,128)} %param.9) | copy-start | bytes 1540
  18.9 16.6 %copy-start.3 = (s32[32,4]{0,1:T(4,128)S(1)}, s32[32,4]{0,1:T(4,128)}, u32[]{:S(2)}) copy-start(s32[32,4]{0,1:T(4,128)} %param.10) | copy-start | bytes 1540
  23.6 108.6 %all-to-all-start = ((bf16[256,64,128]{2,0,1:T(8,128)(2,1)}), bf16[256,64,128]{2,0,1:T(8,128)(2,1)}, u32[]{:S(2)}, u32[]{:S(2)}) async-start(bf16[256,64,128]{2,0,1:T(8,128)(2,1)} %multiply_bitcast_fusion), calls=%async_computation | async-start | bytes 8388608 | tf_op jit(solution)/shard_map/all_to_all | solution.py:36
  35.2 379.5 %all-reduce.3.cloned.1.call-start = ((), (), s32[]{:S(2)}) async-start(), calls=%async_computation.1 | async-start | bytes 524288 | tf_op jit(solution)/shard_map/psum | solution.py:42
  163.8 307.9 %copy-start.1 = (bf16[4,128,512]{2,1,0:T(8,128)(2,1)S(1)}, bf16[4,128,512]{2,1,0:T(8,128)(2,1)}, u32[]{:S(2)}) copy-start(bf16[4,128,512]{2,1,0:T(8,128)(2,1)} %param.11) | copy-start | bytes 1572868
  452.9 18.9 %copy-start.2 = (f32[256,256]{1,0:T(8,128)}, f32[256,256]{1,0:T(8,128)S(1)}, u32[]{:S(2)}) copy-start(f32[256,256]{1,0:T(8,128)S(1)} %select_select_fusion) | copy-start | bytes 786436
Sparse Core Ops, SparseCore 0:
  163.9 250.7 all-reduce.2
where the time goes:
time: 480 us; the launch traced here: 479 us
  waiting for transfers between devices  312 us (65%)
  local copies, waits for them, and re-layouts  56.6 us (12%)
  other arithmetic  50.8 us (11%)
  matrix products  32.2 us (7%)
  between operations  15.5 us (3%)
  starting transfers between devices  11.7 us (2%)
    psum x1, waiting for transfers between devices, body(): gram = lax.psum(gram, ('gx', 'gy'))  246 us
    all_to_all x1, waiting for transfers between devices, body(): lax.all_to_all(outgoing, 'gy', split_axis=1, concat_axis=1, tiled=True)  65.5 us
    another operation x6, other arithmetic, body(): factor = jnp.linalg.cholesky(covariance)  34.2 us
    gather x2, local copies, waits for them, and re-layouts, lift(): chosen = jnp.take(maps, levels, axis=0)  30.7 us
    dot_general x1, matrix products, lift(): jnp.einsum('sbnc,bncd->sbd', picked, chosen, preferred_element_type=jnp.f...  12.8 us
    all_to_all x1, starting transfers between devices, body(): lax.all_to_all(outgoing, 'gy', split_axis=1, concat_axis=1, tiled=True)  11.6 us
    dot_general x1, matrix products, body(): lax.dot_general(bricks, bricks, (((1,), (1,)), ((), ())), preferred_eleme...  9.83 us
    another operation x2, other arithmetic, body(): lax.linalg.triangular_solve(factor[:kept, :kept], bricks[:kept].astype(jn...  9.82 us
  transfers between devices with their start and end apart: 2, of which 2 were waited for; matrix products, arithmetic and copies ran while one was open for 8% of the time, Pallas kernels for 0%

commit v1 on v0

--- a/solution.py
+++ b/solution.py
@@ -39,7 +39,7 @@
         bricks, bricks, (((1,), (1,)), ((), ())), preferred_element_type=jnp.float32
     )
     total_cells = lax.axis_size("gx") * lax.axis_size("gy") * bricks.shape[1]
-    gram = lax.psum(gram, ("gx", "gy"))
+    gram = jnp.sum(lax.all_gather(gram, ("gx", "gy")), axis=0)
     covariance = gram / total_cells
     factor = jnp.linalg.cholesky(covariance)
     kept = RANK

time: 480 us -> 457 us (0.952)
  waiting for transfers between devices: 312 us -> 270 us
  other arithmetic: 50.8 us -> 70.8 us
    psum x1 -> x0, waiting for transfers between devices: 246 us -> none  [body(): gram = lax.psum(gram, ('gx', 'gy'))]
    all_gather x0 -> x1, waiting for transfers between devices: none -> 204 us  [body(): gram = jnp.sum(lax.all_gather(gram, ('gx', 'gy')), axis=0)]
    reduce_sum x0 -> x1, other arithmetic: none -> 21.3 us  [body(): gram = jnp.sum(lax.all_gather(gram, ('gx', 'gy')), axis=0)]
where the time goes in v1:
time: 457 us; the launch traced here: 455 us
  waiting for transfers between devices  270 us (59%)
  other arithmetic  70.8 us (15%)
  local copies, waits for them, and re-layouts  56.5 us (12%)
  matrix products  31.2 us (7%)
  between operations  15.5 us (3%)
  starting transfers between devices  11.7 us (3%)
    all_gather x1, waiting for transfers between devices, body(): gram = jnp.sum(lax.all_gather(gram, ('gx', 'gy')), axis=0)  204 us
    all_to_all x1, waiting for transfers between devices, body(): lax.all_to_all(outgoing, 'gy', split_axis=1, concat_axis=1, tiled=True)  65.6 us
    another operation x6, other arithmetic, body(): factor = jnp.linalg.cholesky(covariance)  33.9 us
    gather x2, local copies, waits for them, and re-layouts, lift(): chosen = jnp.take(maps, levels, axis=0)  30.7 us
    reduce_sum x1, other arithmetic, body(): gram = jnp.sum(lax.all_gather(gram, ('gx', 'gy')), axis=0)  21.3 us
    dot_general x1, matrix products, lift(): jnp.einsum('sbnc,bncd->sbd', picked, chosen, preferred_element_type=jnp.f...  12.8 us
    all_to_all x1, starting transfers between devices, body(): lax.all_to_all(outgoing, 'gy', split_axis=1, concat_axis=1, tiled=True)  11.6 us
    another operation x2, other arithmetic, body(): lax.linalg.triangular_solve(factor[:kept, :kept], bricks[:kept].astype(jn...  10 us
  transfers between devices with their start and end apart: 2, of which 2 were waited for; matrix products, arithmetic and copies ran while one was open for 8% of the time, Pallas kernels for 0%

profile of v1, /device:TPU:2, one launch (start us, length us, event | category | flops | bytes accessed | tf_op | source)
XLA Modules:
  0.0 455.2 jit_solution(18167191509244958377)
XLA Ops:
  7.2 0.0 copy-start
  7.2 0.8 copy.45
  8.0 0.1 reshape.97
  8.1 0.1 reshape.95
  8.2 0.7 fusion.20
  8.9 0.1 reshape.98
  9.1 4.1 copy.46
  13.2 3.2 copy.48
  16.4 3.1 gather_fusion.1
  19.5 0.0 copy-start.3
  19.5 0.0 copy-start.4
  19.5 4.7 %multiply_bitcast_fusion = bf16[256,64,128]{2,0,1:T(8,128)(2,1)} fusion(bf16[64,256,128]{2,1,0:T(8,128)(2,1)} %gather_fusion.1, pred[64]{0:T(512)(128)(4,1)S(1)} %compare_and_fusion, bf16[64]{0:T(256)(128)(2,1)S(1)} %reshape.98), kind=kLoop, calls=%fused_computation.12 | loop fusion | flops 4194304 | bytes 8388800 | tf_op jit(solution)/shard_map/mul | solution.py:35
  24.2 11.6 %all-to-all-start = ((bf16[256,64,128]{2,0,1:T(8,128)(2,1)}), bf16[256,64,128]{2,0,1:T(8,128)(2,1)}, u32[]{:S(2)}, u32[]{:S(2)}) async-start(bf16[256,64,128]{2,0,1:T(8,128)(2,1)} %multiply_bitcast_fusion), calls=%async_computation | async-start | bytes 8388608 | tf_op jit(solution)/shard_map/all_to_all | solution.py:36
  35.8 0.0 all-gather.3.cloned.1.call-start
  35.9 0.0 copy-done.3
  35.9 0.1 copy.41
  36.0 0.0 copy-done.4
  36.0 0.1 copy.44
  36.1 0.1 copy.42
  36.2 0.1 reshape.101
  36.3 0.1 copy.49
  36.4 0.1 reshape.117
  36.6 0.0 copy-done
  36.6 8.1 %gather_fusion = bf16[128,128,512]{2,1,0:T(8,128)(2,1)} fusion(bf16[4,128,512]{2,1,0:T(8,128)(2,1)S(1)} %copy-done, s32[1024]{0:T(1024)S(1)} %pad_clamp_fusion.2), kind=kCustom, calls=%fused_computation | custom fusion | bytes 33554944 | tf_op jit(solution)/shard_map/jit(_take)/gather | solution.py:18
  44.7 22.5 %copy.43 = bf16[32,4,128,512]{2,3,1,0:T(8,128)(2,1)} copy(bf16[32,4,128,512]{3,2,1,0:T(8,128)(2,1)} %bitcast.44) | data formatting | bytes 33554432 | tf_op jit(solution)/shard_map/jit(_take)/gather | solution.py:18
  67.2 65.6 %all-to-all-done = bf16[256,64,128]{2,0,1:T(8,128)(2,1)} async-done(((bf16[256,64,128]{2,0,1:T(8,128)(2,1)}), bf16[256,64,128]{2,0,1:T(8,128)(2,1)}, u32[]{:S(2)}, u32[]{:S(2)}) %all-to-all-start) | async-done | bytes 4194336 | tf_op jit(solution)/shard_map/all_to_all | solution.py:36
  132.8 8.9 %gather_fusion.2 = bf16[128,256,128]{2,1,0:T(8,128)(2,1)} fusion(bf16[256,64,128]{2,0,1:T(8,128)(2,1)} %all-to-all-done, s32[1024]{0:T(1024)S(1)} %pad_clamp_fusion), kind=kCustom, calls=%fused_computation.2 | custom fusion | bytes 16777728 | tf_op jit(solution)/shard_map/jit(_take)/gather | solution.py:17
  141.8 12.8 %fusion.3 = bf16[256,32,512]{0,2,1:T(8,128)(2,1)} fusion(bf16[32,4,256,128]{3,2,1,0:T(8,128)(2,1)} %bitcast.46, pred[32,4]{1,0:T(8,128)(4,1)S(1)} %copy.44, bf16[32,4,128,512]{2,3,1,0:T(8,128)(2,1)} %copy.43, pred[32,4]{1,0:T(8,128)(4,1)S(1)} %copy.41), kind=kOutput, calls=%fused_computation.7 | convolution fusion | flops 4311744512 | bytes 33554688 | tf_op jit(solution)/shard_map/sbnc,bncd->sbd/dot_general | solution.py:19
  154.6 8.8 %convolution_bitcast_fusion = f32[256,256]{1,0:T(8,128)} fusion(bf16[256,32,512]{0,2,1:T(8,128)(2,1)} %fusion.3), kind=kOutput, calls=%fused_computation.14 | convolution fusion | flops 2147483648 | bytes 8650752 | tf_op jit(solution)/shard_map/dot_general | solution.py:38
  163.4 0.0 all-gather.3.cloned.1.call-update
  163.4 4.6 %triangular_solve.20 = bf16[128,32,512]{0,2,1:T(8,128)(2,1)} slice(bf16[256,32,512]{0,2,1:T(8,128)(2,1)} %fusion.3), slice={[0:128], [0:32], [0:512]} | slice | bytes 8388608 | tf_op jit(solution)/shard_map/triangular_solve | solution.py:46
  168.0 203.9 %all-gather.3.cloned.1.call-done = f32[65536,256]{1,0:T(8,128)} async-done(((f32[256,256]{1,0:T(8,128)}), f32[65536,256]{1,0:T(8,128)}) %all-gather.3.cloned.1.call-update) | async-done | bytes 67108880 | tf_op jit(solution)/shard_map/all_gather | solution.py:42
  372.0 0.0 copy-start.1
  372.0 21.3 %reduce_sum.11 = f32[256,256]{1,0:T(8,128)S(1)} reduce(f32[256,256,256]{2,1,0:T(8,128)} %bitcast.10, f32[]{:T(128)} %constant.117.clone.1), dimensions={0}, to_apply=%region_0.1 | reduce | flops 16711680 | bytes 67371008 | tf_op jit(solution)/shard_map/reduce_sum | solution.py:42
  393.2 0.1 copy.52
  393.4 11.7 %cholesky.53 = f32[128,128]{1,0:T(8,128)S(1)} custom-call(f32[128,128]{1,0:T(8,128)S(1)} %cholesky.124), custom_call_target="Cholesky" | custom-call | tf_op jit(solution)/shard_map/jit(cholesky)/cholesky | solution.py:44
  405.2 9.8 %custom-call.14 = f32[1,128,128]{1,2,0:T(8,128)S(1)} custom-call(f32[1,128,128]{2,1,0:T(8,128)S(1)} %get-tuple-element.5), custom_call_target="InvertDiagBlocksLowerTriangular" | custom-call | tf_op jit(solution)/shard_map/jit(cholesky)/cholesky | solution.py:44
  415.0 0.2 constant_dynamic-update-slice_fusion.1
  415.2 0.3 convolution_subtract_fusion
  415.5 11.7 %cholesky.111 = f32[128,128]{1,0:T(8,128)S(1)} custom-call(f32[128,128]{1,0:T(8,128)S(1)} %convolution_subtract_fusion), custom_call_target="Cholesky" | custom-call | tf_op jit(solution)/shard_map/jit(cholesky)/cholesky | solution.py:44
  427.2 0.6 compare_reduce_fusion
  429.2 0.0 copy-start.2
  429.3 10.0 %custom-call.15 = f32[1,128,128]{1,2,0:T(8,128)S(1)} custom-call(f32[1,128,128]{2,1,0:T(8,128)S(1)} %fusion.14), custom_call_target="InvertDiagBlocksLowerTriangular" | custom-call | tf_op jit(solution)/shard_map/triangular_solve | solution.py:46
  439.3 9.1 %fusion.17 = f32[128,16384]{1,0:T(8,128)} fusion(bf16[128,16384]{0,1:T(8,128)(2,1)} %bitcast.45, f32[1,128,128]{1,2,0:T(8,128)S(1)} %custom-call.15), kind=kOutput, calls=%fused_computation.24 | convolution fusion | flops 3221225472 | bytes 12648448 | tf_op jit(solution)/shard_map/triangular_solve | solution.py:46
  448.3 0.0 copy-done.2
  448.3 0.0 copy-done.1
  (16 shorter events, 0.2 us)
Async XLA Ops:
  7.2 29.4 %copy-start = (bf16[4,128,512]{2,1,0:T(8,128)(2,1)S(1)}, bf16[4,128,512]{2,1,0:T(8,128)(2,1)}, u32[]{:S(2)}) copy-start(bf16[4,128,512]{2,1,0:T(8,128)(2,1)} %param.11) | copy-start | bytes 1572868
  19.5 16.4 %copy-start.3 = (s32[32,4]{0,1:T(4,128)S(1)}, s32[32,4]{0,1:T(4,128)}, u32[]{:S(2)}) copy-start(s32[32,4]{0,1:T(4,128)} %param.10) | copy-start | bytes 1540
  19.5 16.5 %copy-start.4 = (s32[32,4]{0,1:T(4,128)S(1)}, s32[32,4]{0,1:T(4,128)}, u32[]{:S(2)}) copy-start(s32[32,4]{0,1:T(4,128)} %param.9) | copy-start | bytes 1540
  24.2 108.6 %all-to-all-start = ((bf16[256,64,128]{2,0,1:T(8,128)(2,1)}), bf16[256,64,128]{2,0,1:T(8,128)(2,1)}, u32[]{:S(2)}, u32[]{:S(2)}) async-start(bf16[256,64,128]{2,0,1:T(8,128)(2,1)} %multiply_bitcast_fusion), calls=%async_computation | async-start | bytes 8388608 | tf_op jit(solution)/shard_map/all_to_all | solution.py:36
  35.8 336.1 %all-gather.3.cloned.1.call-start = ((), (), s32[]{:S(2)}) async-start(), calls=%async_computation.1 | async-start | bytes 67371008 | tf_op jit(solution)/shard_map/all_gather | solution.py:42
  372.0 76.4 %copy-start.1 = (bf16[4,128,512]{2,1,0:T(8,128)(2,1)S(1)}, bf16[4,128,512]{2,1,0:T(8,128)(2,1)}, u32[]{:S(2)}) copy-start(bf16[4,128,512]{2,1,0:T(8,128)(2,1)} %param.11) | copy-start | bytes 1572868
  429.2 19.1 %copy-start.2 = (f32[256,256]{1,0:T(8,128)}, f32[256,256]{1,0:T(8,128)S(1)}, u32[]{:S(2)}) copy-start(f32[256,256]{1,0:T(8,128)S(1)} %select_select_fusion) | copy-start | bytes 786436
Sparse Core Ops, SparseCore 0:
  163.6 208.3 all-gather.2
